TPU v7x, 32 devices: a whole 2x2x4 slice. The times are simulated.
32 devices in a mesh: sample: 16 (over z, x, core), block: 2 (over y).
Axes of the slice: x: 2, y: 2, z: 4, core: 2. Of those that a mesh axis runs over, the one named last changes fastest.
Arguments:
- genotype: int32 [16384, 2000], P('sample', 'block'), may hold values from 0 to 2
- allele_freq: float32 [2000], P('block'), may hold values from 0.05 to 0.5
- phenotype: bfloat16 [16384, 16], P('sample'), may hold values from -6 to 6
- shrinkage: float32 [2], replicated, may hold values from 0.05 to 2
- owner_order: int32 [16], replicated, may hold values from 0 to 15, each once
Outputs:
- predictions: bfloat16 [16, 8, 16384], P('block', None, 'sample')
Inputs may be any that keep to these rules, and one draw needn't show every extreme that they name: `owner_order`: each phenotype appears once.
All inputs are finite; a program needn't handle non-finite values.
Results may differ from a plain program's by a relative error of at most 0.0056.
Values may be sent and summed in bfloat16 or wider, within the bound.
No kernel may reach another device: no remote copies, remote signals or barrier semaphores. Data moves between devices by JAX's collectives and lax.ppermute only.
A program may use at most 128 MiB of HBM per device.

v0:
```python
import jax
import jax.numpy as jnp
from jax import lax
from jax.sharding import PartitionSpec as P

SNPS = 500
FOLDS = 5
PANEL = 128
HIGH = lax.Precision.HIGHEST


def standardize(genotype, allele_freq):
    spread = jnp.sqrt(2.0 * allele_freq * (1.0 - allele_freq))
    return ((genotype.astype(jnp.float32) - 2.0 * allele_freq) / spread).astype(jnp.bfloat16)


def predict(columns, weights):
    stacked = jnp.transpose(weights, (2, 0, 1)).reshape(-1, weights.shape[1])
    product = lax.dot_general(
        stacked, columns, (((1,), (1,)), ((), ())), preferred_element_type=jnp.float32
    )
    return product.astype(jnp.bfloat16).reshape(
        weights.shape[2], weights.shape[0], columns.shape[0]
    )


def inner_products(left_cols, right_cols):
    return lax.dot_general(
        left_cols, right_cols, (((0,), (0,)), ((), ())), preferred_element_type=jnp.float32
    )


def tile_pairs(panels):
    pairs = []
    for row_tile in range(panels):
        for col_tile in range(row_tile, panels):
            pairs.append((row_tile, col_tile))
    return pairs


def tile_grams(left_cols, right_cols, panels):
    tile_list = []
    for row_tile, col_tile in tile_pairs(panels):
        first = left_cols[:, row_tile * PANEL : (row_tile + 1) * PANEL]
        second = right_cols[:, col_tile * PANEL : (col_tile + 1) * PANEL]
        tile_list.append(inner_products(first, second))
    return jnp.stack(tile_list)


def mm(spec, left, right):
    return jnp.einsum(spec, left, right, precision=HIGH, preferred_element_type=jnp.float32)


def block_solve(tiles, target, panels):
    pairs = tile_pairs(panels)
    upper = {pair: tiles[:, index] for index, pair in enumerate(pairs)}
    eye = jnp.broadcast_to(jnp.eye(PANEL, dtype=jnp.float32), (tiles.shape[0], PANEL, PANEL))
    lower = {}
    inverse = {}
    for p in range(panels):
        factor = jnp.linalg.cholesky(upper[p, p])
        inv = lax.linalg.triangular_solve(factor, eye, left_side=True, lower=True)
        inverse[p] = inv
        for q in range(p + 1, panels):
            lower[q, p] = mm("sji,skj->sik", upper[p, q], inv)
        for r in range(p + 1, panels):
            for q in range(r, panels):
                upper[r, q] = upper[r, q] - mm("sik,sjk->sij", lower[r, p], lower[q, p])
    forward = []
    for p in range(panels):
        rhs = target[:, p * PANEL : (p + 1) * PANEL]
        for q in range(p):
            rhs = rhs - mm("sij,sjc->sic", lower[p, q], forward[q])
        forward.append(mm("sij,sjc->sic", inverse[p], rhs))
    backward = [None] * panels
    for p in reversed(range(panels)):
        rhs = forward[p]
        for q in range(p + 1, panels):
            rhs = rhs - mm("sji,sjc->sic", lower[q, p], backward[q])
        backward[p] = mm("sji,sjc->sic", inverse[p], rhs)
    return jnp.concatenate(backward, axis=1)


def shared_solve(summed_grams, summed_crosses, shrinkage, counts, panels):
    member_count = summed_grams.shape[1]
    ridge_count = shrinkage.shape[0]
    systems = FOLDS * member_count * ridge_count
    devices = lax.axis_size("sample")
    share = -(-systems // devices)
    owned_ids = lax.axis_index("sample") * share + lax.broadcasted_iota(jnp.int32, (share,), 0)
    owned_ids = jnp.minimum(owned_ids, systems - 1)
    pair_ids = owned_ids // ridge_count
    ridge_ids = owned_ids % ridge_count
    fold_ids = pair_ids // member_count
    member_ids = pair_ids % member_count
    fold_axis = jnp.arange(FOLDS, dtype=jnp.int32)[:, None, None]
    member_axis = jnp.arange(member_count, dtype=jnp.int32)[None, :, None]
    keep = jnp.logical_and(
        fold_axis != fold_ids[None, None, :], member_axis == member_ids[None, None, :]
    )
    keep = keep.astype(jnp.float32)
    rest_tiles = jnp.einsum("kms,kmtij->stij", keep, summed_grams, precision=HIGH)
    rest_crosses = jnp.einsum("kms,kmic->sic", keep, summed_crosses, precision=HIGH)
    chosen_counts = jnp.take(counts, fold_ids, axis=0)
    ridge = jnp.take(shrinkage, ridge_ids, axis=0)
    width = rest_tiles.shape[-1]
    diag_ids = [
        index
        for index, (row_tile, col_tile) in enumerate(tile_pairs(panels))
        if row_tile == col_tile
    ]
    is_diag = jnp.zeros((len(tile_pairs(panels)),), jnp.float32).at[jnp.array(diag_ids)].set(1.0)
    position = lax.broadcasted_iota(jnp.int32, (panels, width), 1) + PANEL * lax.broadcasted_iota(
        jnp.int32, (panels, width), 0
    )
    padded = (position >= SNPS).astype(jnp.float32)
    pad_diag = (
        jnp.zeros((len(tile_pairs(panels)), width), jnp.float32).at[jnp.array(diag_ids)].set(padded)
    )
    identity = jnp.eye(width, dtype=jnp.float32)
    diag_add = (
        ridge[:, None, None] * is_diag[None, :, None]
        + (1.0 - ridge[:, None, None]) * pad_diag[None, :, :]
    )
    system = rest_tiles / chosen_counts[:, None, None, None] + diag_add[:, :, :, None] * identity
    target = rest_crosses / chosen_counts[:, None, None]
    solved = block_solve(system, target, panels)[:, :SNPS].astype(jnp.bfloat16)
    collected = lax.all_gather(solved, "sample", axis=0, tiled=True)
    return collected[:systems].reshape(FOLDS, member_count, ridge_count, SNPS, -1)


def shards(genotype, allele_freq, phenotype, shrinkage, owner_order):
    sample_rows = genotype.shape[0]
    total_rows = sample_rows * lax.axis_size("sample")
    scaled = standardize(genotype, allele_freq)
    ordered = jnp.take(phenotype, owner_order, axis=1)
    local_blocks = allele_freq.shape[0] // SNPS
    panels = -(-SNPS // PANEL)
    padded_width = panels * PANEL
    column_sets = [scaled[:, member * SNPS : (member + 1) * SNPS] for member in range(local_blocks)]
    bounds = [-(-(k * total_rows) // FOLDS) for k in range(FOLDS + 1)]
    counts = jnp.array(
        [float(total_rows - (bounds[k + 1] - bounds[k])) for k in range(FOLDS)], dtype=jnp.float32
    )
    start_row = lax.axis_index("sample") * sample_rows
    row_ids = start_row + lax.broadcasted_iota(jnp.int32, (sample_rows,), 0)
    fold_of = row_ids * FOLDS // total_rows
    first_fold = start_row * FOLDS // total_rows
    slot_folds = [first_fold, first_fold + 1]
    slot_masks = [fold_of == slot_folds[0], fold_of == slot_folds[1]]
    picked = jnp.minimum(jnp.stack(slot_folds), FOLDS - 1)
    fold_ids = jnp.arange(FOLDS, dtype=jnp.int32)
    tile_count = len(tile_pairs(panels))

    def fold_partials(member):
        columns = jnp.pad(column_sets[member], ((0, 0), (0, padded_width - SNPS)))
        gram_total = jnp.zeros((FOLDS, tile_count, PANEL, PANEL), jnp.float32)
        cross_total = jnp.zeros((FOLDS, padded_width, ordered.shape[1]), jnp.float32)
        for slot in range(2):
            masked = jnp.where(slot_masks[slot][:, None], columns, jnp.zeros_like(columns))
            selector = (fold_ids == slot_folds[slot]).astype(jnp.float32)
            gram_total = (
                gram_total
                + selector[:, None, None, None] * tile_grams(masked, columns, panels)[None]
            )
            cross_total = (
                cross_total + selector[:, None, None] * inner_products(masked, ordered)[None]
            )
        return (gram_total, cross_total)

    def weights_for(members):
        parts = [fold_partials(member) for member in members]
        grams = jnp.stack([item[0] for item in parts], axis=1)
        crosses = jnp.stack([item[1] for item in parts], axis=1)
        summed_grams, summed_crosses = lax.psum((grams, crosses), "sample")
        every_weights = shared_solve(summed_grams, summed_crosses, shrinkage, counts, panels)
        return jnp.take(every_weights, picked, axis=0)

    def fold_predictions(member, slot_weights):
        columns = column_sets[member]
        lower = predict(columns, slot_weights[0])
        upper = predict(columns, slot_weights[1])
        return jnp.where(slot_masks[1][None, None, :], upper, lower)

    weights = weights_for(list(range(local_blocks)))
    local_preds = jnp.concatenate(
        [fold_predictions(member, weights[:, member]) for member in range(local_blocks)], axis=1
    )
    return lax.all_to_all(local_preds, "block", split_axis=0, concat_axis=1, tiled=True)


def solution(mesh):
    in_specs = (P("sample", "block"), P("block"), P("sample", None), P(), P())
    out_specs = P("block", None, "sample")
    return jax.shard_map(shards, mesh=mesh, in_specs=in_specs, out_specs=out_specs, check_vma=False)
```

profile of v0, /device:TPU:0, one launch (start us, length us, event | category | flops | bytes accessed | tf_op | source)
XLA Modules:
  0.0 510.8 jit_solution(4476587535390059192)
XLA Ops:
  6.5 0.7 compare_and_fusion
  7.2 0.7 compare_select_fusion.1
  7.9 0.7 broadcast_multiply_fusion.1
  8.6 2.7 divide_convert_fusion
  11.6 0.6 gather_fusion.2
  12.6 0.4 fusion.151
  13.0 1.0 broadcast_select_fusion.2
  14.4 0.4 fusion.153
  24.4 0.9 pad_maximum_fusion.1
  25.3 1.4 multiply_add_fusion.1
  26.7 4.9 pad_maximum_fusion
  31.7 0.7 copy.156
  32.4 0.6 gather_fusion
  33.1 0.6 gather_fusion.1
  33.7 0.9 scatter_custom_fusion
  34.6 0.7 compare_and_fusion.1
  35.4 0.6 pad_clamp_fusion
  36.1 0.6 and_select_fusion.5
  36.8 0.7 multiply_add_fusion.5
  37.5 205.3 %all-reduce.4.cloned.1.call-done = (f32[5,2,10,128,128]{4,0,1,3,2:T(8,128)}, f32[5,2,512,16]{2,0,1,3:T(8,128)}) async-done(((f32[5,2,10,128,128]{4,0,1,3,2:T(8,128)}, f32[5,2,512,16]{2,0,1,3:T(8,128)}), (f32[5,2,10,128,128]{4,0,1,3,2:T(8,128)}, f32[5,2,512,16]{2,0,1,3:T(8,128)})) %all-reduce.4.cloned.1.call-update) | async-done | bytes 6881296 | tf_op jit(solution)/shard_map/psum | solution.py:175
  242.8 10.3 %convolution_bitcast_fusion = f32[2,10,128,128]{3,0,2,1:T(2,128)S(1)} fusion(f32[5,2,10,128,128]{4,0,1,3,2:T(8,128)} %get-tuple-element.6, pred[2,2]{1,0:T(4,128)(4,1)S(1)} %iota_compare_fusion.3, pred[5,2]{0,1:T(4,128)(4,1)S(1)} %iota_compare_fusion.4), kind=kOutput, calls=%fused_computation.9 | convolution fusion | flops 39321620 | bytes 7864334 | tf_op jit(solution)/shard_map/kms,kmtij->stij/dot_general | solution.py:102
  253.1 2.6 copy.154
  255.7 1.7 multiply_add_fusion.2
  257.4 0.7 slice_bitcast_fusion.12
  258.1 1.7 copy.155
  259.8 1.6 fusion.97
  261.4 24.9 %custom-call.12 = f32[2,128,128]{2,1,0:T(8,128)} custom-call(f32[2,128,128]{2,1,0:T(8,128)} %fusion.97), custom_call_target="Cholesky" | custom-call | tf_op jit(solution)/shard_map/jit(cholesky)/cholesky | solution.py:61
  286.3 0.9 select_reduce_fusion.3
  287.3 1.6 select_bitcast_fusion.3
  289.0 21.1 %custom-call.13 = f32[2,1,128,128]{2,3,1,0:T(8,128)} custom-call(f32[2,1,128,128]{3,2,1,0:T(8,128)} %select_bitcast_fusion.3), custom_call_target="InvertDiagBlocksLowerTriangular" | custom-call | tf_op jit(solution)/shard_map/triangular_solve/custom-call.0 | solution.py:62
  310.1 1.3 fusion.107
  311.8 1.4 fusion.95
  313.2 1.3 fusion.96
  314.5 1.5 convolution_bitcast_fusion.1
  316.0 0.7 copy_divide_fusion
  317.1 1.3 convolution_subtract_fusion.9
  319.0 0.4 convolution_subtract_fusion.4
  319.4 0.9 convolution_subtract_fusion.20
  320.4 0.4 convolution_subtract_fusion.8
  320.8 1.1 convolution_subtract_fusion.5
  322.2 0.4 convolution_subtract_fusion.2
  322.8 23.9 %custom-call.14 = f32[2,128,128]{2,1,0:T(8,128)S(1)} custom-call(f32[2,128,128]{2,1,0:T(8,128)S(1)} %fusion.106), custom_call_target="Cholesky" | custom-call | tf_op jit(solution)/shard_map/jit(cholesky)/cholesky | solution.py:61
  346.9 19.7 %custom-call.15 = f32[2,1,128,128]{2,3,1,0:T(8,128)S(1)} custom-call(f32[2,1,128,128]{3,2,1,0:T(8,128)S(1)} %select_bitcast_fusion.2), custom_call_target="InvertDiagBlocksLowerTriangular" | custom-call | tf_op jit(solution)/shard_map/triangular_solve/custom-call.0 | solution.py:62
  367.3 0.4 fusion.163
  367.7 0.4 fusion.161
  368.1 0.9 convolution_subtract_fusion.17
  369.0 1.0 convolution_subtract_fusion.19
  370.0 1.3 convolution_subtract_fusion.3
  371.7 1.1 convolution_subtract_fusion.1
  372.9 23.5 %custom-call.16 = f32[2,128,128]{2,1,0:T(8,128)S(1)} custom-call(f32[2,128,128]{2,1,0:T(8,128)S(1)} %fusion.103), custom_call_target="Cholesky" | custom-call | tf_op jit(solution)/shard_map/jit(cholesky)/cholesky | solution.py:61
  396.6 19.8 %custom-call.17 = f32[2,1,128,128]{2,3,1,0:T(8,128)S(1)} custom-call(f32[2,1,128,128]{3,2,1,0:T(8,128)S(1)} %select_bitcast_fusion.1), custom_call_target="InvertDiagBlocksLowerTriangular" | custom-call | tf_op jit(solution)/shard_map/triangular_solve/custom-call.0 | solution.py:62
  417.6 1.3 convolution_subtract_fusion
  418.9 0.8 copy.173
  419.7 1.6 fusion.100
  421.2 24.3 %custom-call.18 = f32[2,128,128]{2,1,0:T(8,128)S(1)} custom-call(f32[2,128,128]{2,1,0:T(8,128)} %fusion.100), custom_call_target="Cholesky" | custom-call | tf_op jit(solution)/shard_map/jit(cholesky)/cholesky | solution.py:61
  445.7 0.7 select_bitcast_fusion
  446.4 20.5 %custom-call.19 = f32[2,1,128,128]{2,3,1,0:T(8,128)S(1)} custom-call(f32[2,1,128,128]{3,2,1,0:T(8,128)} %select_bitcast_fusion), custom_call_target="InvertDiagBlocksLowerTriangular" | custom-call | tf_op jit(solution)/shard_map/triangular_solve/custom-call.0 | solution.py:62
  467.3 1.0 convolution_subtract_fusion.16
  471.0 21.9 %all_gather.3 = bf16[32,500,16]{1,2,0:T(8,128)(2,1)S(1)} all-gather(bf16[2,500,16]{1,2,0:T(8,128)(2,1)S(1)} %pad_maximum_fusion.3), channel_id=1, replica_groups=mesh['sample'=16,'block'=2] {'sample'}, dimensions={0}, use_global_device_ids=true | all-gather | bytes 544000 | tf_op jit(solution)/shard_map/all_gather | solution.py:128
  493.0 0.7 gather_fusion.3
  494.3 0.4 convolution_convert_fusion
  494.8 0.4 convolution_convert_fusion.1
  496.0 7.0 %all_to_all.18 = bf16[16,4,1024]{2,1,0:T(4,128)(2,1)S(1)} all-to-all(bf16[16,4,1024]{2,1,0:T(4,128)(2,1)S(1)} %pad_maximum_fusion.2), channel_id=1, replica_groups=mesh['sample'=16,'block'=2] {'block'}, dimensions={0} | all-to-all | bytes 262144 | tf_op jit(solution)/shard_map/all_to_all | solution.py:189
  503.0 0.7 all_to_all.16
  (153 shorter events, 20.3 us)
Async XLA Ops:
  6.5 5.1 copy-start
  6.5 236.2 %all-reduce.4.cloned.1.call-start = ((), (), s32[]{:S(2)}) async-start(), calls=%async_computation.1 | async-start | bytes 22020096 | tf_op jit(solution)/shard_map/psum | solution.py:175
  7.9 5.1 copy-start.10
  12.2 0.8 copy-start.15
  31.6 0.8 copy-start.2
  31.6 1.5 copy-start.1
  31.6 5.1 %copy-start.16 = (f32[10]{0:T(128)S(1)}, f32[10]{0:T(128)}, u32[]{:S(2)}) copy-start(f32[10]{0:T(128)} %constant.196) | copy-start | bytes 124
  31.7 211.1 %copy-start.9 = (f32[128,128]{0,1:T(8,128)}, f32[128,128]{0,1:T(8,128)S(1)}, u32[]{:S(2)}) copy-start(f32[128,128]{0,1:T(8,128)S(1)} %fusion.125) | copy-start | bytes 196612
  36.0 217.1 %copy-start.12 = (pred[2,2]{1,0:T(4,128)(4,1)}, pred[2,2]{1,0:T(4,128)(4,1)S(1)}, u32[]{:S(2)}) copy-start(pred[2,2]{1,0:T(4,128)(4,1)S(1)} %iota_compare_fusion.3) | copy-start | bytes 16
  36.1 217.0 %copy-start.13 = (pred[5,2]{0,1:T(4,128)(4,1)}, pred[5,2]{0,1:T(4,128)(4,1)S(1)}, u32[]{:S(2)}) copy-start(pred[5,2]{0,1:T(4,128)(4,1)S(1)} %iota_compare_fusion.4) | copy-start | bytes 34
  255.7 54.3 %copy-start.7 = (f32[128,128]{1,0:T(8,128)S(1)}, f32[128,128]{1,0:T(8,128)}, u32[]{:S(2)}) copy-start(f32[128,128]{1,0:T(8,128)} %copy.156) | copy-start | bytes 196612
  257.4 53.9 %copy-start.3 = (f32[2,10,128,128]{2,3,0,1:T(8,128)}, f32[2,10,128,128]{2,3,0,1:T(8,128)S(1)}, u32[]{:S(2)}) copy-start(f32[2,10,128,128]{2,3,0,1:T(8,128)S(1)} %multiply_add_fusion.2) | copy-start | bytes 3932164
  311.4 9.4 %copy-start.5 = (f32[2,128,128]{2,1,0:T(8,128)}, f32[2,128,128]{2,1,0:T(8,128)S(1)}, u32[]{:S(2)}) copy-start(f32[2,128,128]{2,1,0:T(8,128)S(1)} %fusion.107) | copy-start | bytes 393220
  311.8 7.3 %copy-start.4 = (f32[2,10,128,128]{2,3,0,1:T(8,128)S(1)}, f32[2,10,128,128]{2,3,0,1:T(8,128)}, u32[]{:S(2)}) copy-start(f32[2,10,128,128]{2,3,0,1:T(8,128)} %copy-done.3) | copy-start | bytes 3932164
  318.7 47.9 %copy-start.8 = (f32[128,128]{1,0:T(8,128)S(1)}, f32[128,128]{1,0:T(8,128)}, u32[]{:S(2)}) copy-start(f32[128,128]{1,0:T(8,128)} %copy.156) | copy-start | bytes 196612
  417.3 53.5 %copy-start.6 = (f32[2,128,128]{2,1,0:T(8,128)S(1)}, f32[2,128,128]{2,1,0:T(8,128)}, u32[]{:S(2)}) copy-start(f32[2,128,128]{2,1,0:T(8,128)} %copy-done.5) | copy-start | bytes 393220
  470.0 23.6 %copy-start.14 = (pred[2]{0:T(512)(128)(4,1)S(1)}, pred[2]{0:T(512)(128)(4,1)}, u32[]{:S(2)}) copy-start(pred[2]{0:T(512)(128)(4,1)} %compare_and_fusion.1) | copy-start | bytes 10
  494.8 0.9 copy-start.11
Sparse Core Ops, SparseCore 0:
  31.8 210.9 all-reduce.3
where the time goes:
time: 518 us; the launch traced here: 511 us
  waiting for transfers between devices  205 us (40%)
  other arithmetic  204 us (39%)
  matrix products  46.8 us (9%)
  blocking collectives  28.9 us (6%)
  between operations  14.5 us (3%)
  local copies, waits for them, and re-layouts  10.7 us (2%)
    psum x1, waiting for transfers between devices, weights_for(): summed_grams, summed_crosses = lax.psum((grams, crosses), 'sample')  205 us
    another operation x13, other arithmetic, block_solve(): factor = jnp.linalg.cholesky(upper[p, p])  98 us
    another operation x9, other arithmetic, block_solve(): inv = lax.linalg.triangular_solve(factor, eye, left_side=True, lower=True)  83.7 us
    all_gather x1, blocking collectives, shared_solve(): collected = lax.all_gather(solved, 'sample', axis=0, tiled=True)  21.9 us
    dot_general x36, matrix products, mm(): jnp.einsum(spec, left, right, precision=HIGH, preferred_element_type=jnp....  20.4 us
    dot_general x44, matrix products, inner_products(): lax.dot_general(left_cols, right_cols, (((0,), (0,)), ((), ())), preferre...  10.8 us
  transfers between devices with their start and end apart: 1, of which 1 were waited for; matrix products, arithmetic and copies ran while one was open for 1% of the time, Pallas kernels for 0%

commit v1 on v0

--- a/solution.py
+++ b/solution.py
@@ -7,6 +7,19 @@
 FOLDS = 5
 PANEL = 128
 HIGH = lax.Precision.HIGHEST
+
+
+def ring_gather(value, axis, dim):
+    ways = lax.axis_size(axis)
+    up = [(d, (d + 1) % ways) for d in range(ways)]
+    down = [(d, (d - 1) % ways) for d in range(ways)]
+    earlier, later = ([value], [value])
+    for _ in range(ways // 2):
+        earlier.append(lax.ppermute(earlier[-1], axis, up))
+    for _ in range((ways - 1) // 2):
+        later.append(lax.ppermute(later[-1], axis, down))
+    line = jnp.concatenate([*earlier[::-1], *later[1:]], axis=dim)
+    return jnp.roll(line, (lax.axis_index(axis) - ways // 2) * value.shape[dim], axis=dim)
 
 
 def standardize(genotype, allele_freq):
@@ -125,7 +138,7 @@
     system = rest_tiles / chosen_counts[:, None, None, None] + diag_add[:, :, :, None] * identity
     target = rest_crosses / chosen_counts[:, None, None]
     solved = block_solve(system, target, panels)[:, :SNPS].astype(jnp.bfloat16)
-    collected = lax.all_gather(solved, "sample", axis=0, tiled=True)
+    collected = ring_gather(solved, "sample", 0)
     return collected[:systems].reshape(FOLDS, member_count, ridge_count, SNPS, -1)
 
 

time: 518 us -> 546 us (1.054)
  starting transfers between devices: 0.01 us -> 31.4 us
  blocking collectives: 28.9 us -> 7.01 us
  waiting for transfers between devices: 205 us -> 224 us
    ppermute x0 -> x15, starting transfers between devices: none -> 31.4 us  [the longest x7 31.1 us: ring_gather(): later.append(lax.ppermute(later[-1], axis, down))]
    all_gather x1 -> x0, blocking collectives: 21.9 us -> none  [shared_solve(): collected = lax.all_gather(solved, 'sample', axis=0, tiled=True)]
    ppermute x0 -> x15, waiting for transfers between devices: none -> 17.1 us  [the longest x8 17.1 us: ring_gather(): earlier.append(lax.ppermute(earlier[-1], axis, up))]
  transfers between devices with their start and end apart: 1 -> 16, of which waited for: 1 -> 9; matrix products, arithmetic and copies ran while one was open for 1% -> 1% of each run, Pallas kernels for 0% -> 0%
where the time goes in v1:
time: 546 us; the launch traced here: 539 us
  waiting for transfers between devices  224 us (41%)
  other arithmetic  204 us (37%)
  matrix products  46.8 us (9%)
  starting transfers between devices  31.4 us (6%)
  between operations  14.8 us (3%)
  local copies, waits for them, and re-layouts  10.9 us (2%)
  blocking collectives  7.01 us (1%)
    psum x1, waiting for transfers between devices, weights_for(): summed_grams, summed_crosses = lax.psum((grams, crosses), 'sample')  207 us
    another operation x13, other arithmetic, block_solve(): factor = jnp.linalg.cholesky(upper[p, p])  98 us
    another operation x9, other arithmetic, block_solve(): inv = lax.linalg.triangular_solve(factor, eye, left_side=True, lower=True)  83.7 us
    ppermute x7, starting transfers between devices, ring_gather(): later.append(lax.ppermute(later[-1], axis, down))  31.1 us
    dot_general x36, matrix products, mm(): jnp.einsum(spec, left, right, precision=HIGH, preferred_element_type=jnp....  20.4 us
    ppermute x8, waiting for transfers between devices, ring_gather(): earlier.append(lax.ppermute(earlier[-1], axis, up))  17.1 us
  transfers between devices with their start and end apart: 16, of which 9 were waited for; matrix products, arithmetic and copies ran while one was open for 1% of the time, Pallas kernels for 0%

profile of v1, /device:TPU:0, one launch (start us, length us, event | category | flops | bytes accessed | tf_op | source)
XLA Modules:
  0.0 538.5 jit_solution(6331177492002957270)
XLA Ops:
  6.5 0.7 compare_and_fusion
  7.2 0.7 compare_select_fusion.1
  7.9 0.7 broadcast_multiply_fusion.1
  8.6 2.7 divide_convert_fusion
  13.6 1.0 broadcast_select_fusion.2
  25.1 0.8 pad_maximum_fusion.1
  25.9 1.4 multiply_add_fusion.1
  27.3 4.9 pad_maximum_fusion
  32.3 0.7 copy.121
  33.7 0.6 gather_fusion
  34.4 0.9 scatter_custom_fusion
  36.1 0.7 multiply_add_fusion.5
  36.8 206.6 %all-reduce.4.cloned.1.call-done = (f32[5,2,10,128,128]{4,0,1,3,2:T(8,128)}, f32[5,2,512,16]{2,0,1,3:T(8,128)}) async-done(((f32[5,2,10,128,128]{4,0,1,3,2:T(8,128)}, f32[5,2,512,16]{2,0,1,3:T(8,128)}), (f32[5,2,10,128,128]{4,0,1,3,2:T(8,128)}, f32[5,2,512,16]{2,0,1,3:T(8,128)})) %all-reduce.4.cloned.1.call-update) | async-done | bytes 6881296 | tf_op jit(solution)/shard_map/psum | solution.py:188
  243.4 10.3 %convolution_bitcast_fusion = f32[2,10,128,128]{3,0,2,1:T(2,128)S(1)} fusion(f32[5,2,10,128,128]{4,0,1,3,2:T(8,128)} %get-tuple-element.6, pred[2,2]{1,0:T(4,128)(4,1)S(1)} %iota_compare_fusion.3, pred[5,2]{0,1:T(4,128)(4,1)S(1)} %iota_compare_fusion.4), kind=kOutput, calls=%fused_computation.9 | convolution fusion | flops 39321620 | bytes 7864334 | tf_op jit(solution)/shard_map/kms,kmtij->stij/dot_general | solution.py:115
  253.8 2.6 copy.119
  256.4 1.7 multiply_add_fusion.2
  258.1 0.7 slice_bitcast_fusion.12
  258.8 1.7 copy.120
  260.4 1.6 fusion.97
  262.0 24.9 %custom-call.12 = f32[2,128,128]{2,1,0:T(8,128)} custom-call(f32[2,128,128]{2,1,0:T(8,128)} %fusion.97), custom_call_target="Cholesky" | custom-call | tf_op jit(solution)/shard_map/jit(cholesky)/cholesky | solution.py:74
  286.9 0.9 select_reduce_fusion.3
  288.0 1.6 select_bitcast_fusion.3
  289.6 21.1 %custom-call.13 = f32[2,1,128,128]{2,3,1,0:T(8,128)} custom-call(f32[2,1,128,128]{3,2,1,0:T(8,128)} %select_bitcast_fusion.3), custom_call_target="InvertDiagBlocksLowerTriangular" | custom-call | tf_op jit(solution)/shard_map/triangular_solve/custom-call.0 | solution.py:75
  310.7 1.3 fusion.107
  312.4 1.4 fusion.95
  313.8 1.3 fusion.96
  315.1 1.5 convolution_bitcast_fusion.1
  316.7 0.7 copy_divide_fusion
  317.7 1.3 convolution_subtract_fusion.9
  320.0 0.9 convolution_subtract_fusion.20
  321.4 1.1 convolution_subtract_fusion.5
  323.3 23.9 %custom-call.14 = f32[2,128,128]{2,1,0:T(8,128)S(1)} custom-call(f32[2,128,128]{2,1,0:T(8,128)S(1)} %fusion.106), custom_call_target="Cholesky" | custom-call | tf_op jit(solution)/shard_map/jit(cholesky)/cholesky | solution.py:74
  347.5 19.7 %custom-call.15 = f32[2,1,128,128]{2,3,1,0:T(8,128)S(1)} custom-call(f32[2,1,128,128]{3,2,1,0:T(8,128)S(1)} %select_bitcast_fusion.2), custom_call_target="InvertDiagBlocksLowerTriangular" | custom-call | tf_op jit(solution)/shard_map/triangular_solve/custom-call.0 | solution.py:75
  368.6 0.9 convolution_subtract_fusion.17
  369.6 1.0 convolution_subtract_fusion.19
  370.6 1.3 convolution_subtract_fusion.3
  372.3 1.1 convolution_subtract_fusion.1
  373.5 23.5 %custom-call.16 = f32[2,128,128]{2,1,0:T(8,128)S(1)} custom-call(f32[2,128,128]{2,1,0:T(8,128)S(1)} %fusion.103), custom_call_target="Cholesky" | custom-call | tf_op jit(solution)/shard_map/jit(cholesky)/cholesky | solution.py:74
  397.2 19.8 %custom-call.17 = f32[2,1,128,128]{2,3,1,0:T(8,128)S(1)} custom-call(f32[2,1,128,128]{3,2,1,0:T(8,128)S(1)} %select_bitcast_fusion.1), custom_call_target="InvertDiagBlocksLowerTriangular" | custom-call | tf_op jit(solution)/shard_map/triangular_solve/custom-call.0 | solution.py:75
  418.2 1.3 convolution_subtract_fusion
  419.5 0.8 copy.138
  420.2 1.6 fusion.100
  421.8 24.3 %custom-call.18 = f32[2,128,128]{2,1,0:T(8,128)S(1)} custom-call(f32[2,128,128]{2,1,0:T(8,128)} %fusion.100), custom_call_target="Cholesky" | custom-call | tf_op jit(solution)/shard_map/jit(cholesky)/cholesky | solution.py:74
  446.2 0.7 select_bitcast_fusion
  447.0 20.5 %custom-call.19 = f32[2,1,128,128]{2,3,1,0:T(8,128)S(1)} custom-call(f32[2,1,128,128]{3,2,1,0:T(8,128)} %select_bitcast_fusion), custom_call_target="InvertDiagBlocksLowerTriangular" | custom-call | tf_op jit(solution)/shard_map/triangular_solve/custom-call.0 | solution.py:75
  467.9 1.0 convolution_subtract_fusion.16
  471.6 6.0 %collective-permute-done = bf16[2,500,16]{1,2,0:T(8,128)(2,1)S(1)} collective-permute-done((bf16[2,500,16]{1,2,0:T(8,128)(2,1)S(1)}, bf16[2,500,16]{1,2,0:T(8,128)(2,1)S(1)}, u32[]{:S(2)}, u32[]{:S(2)}) %collective-permute-start) | collective-permute-done | bytes 32032 | tf_op jit(solution)/shard_map/ppermute | solution.py:18
  477.7 4.4 collective-permute-start.8
  482.1 1.7 collective-permute-done.1
  483.8 4.4 collective-permute-start.9
  488.2 1.6 collective-permute-done.2
  489.8 4.4 collective-permute-start.10
  494.3 1.6 collective-permute-done.3
  495.9 4.4 collective-permute-start.11
  500.3 1.6 collective-permute-done.4
  501.9 4.4 collective-permute-start.12
  506.3 1.6 collective-permute-done.5
  508.2 4.4 collective-permute-start.13
  512.6 1.6 collective-permute-done.6
  514.3 4.5 collective-permute-start.14
  518.8 1.5 collective-permute-done.7
  520.7 0.7 gather_fusion.3
  523.7 7.0 %all_to_all.18 = bf16[16,4,1024]{2,1,0:T(4,128)(2,1)S(1)} all-to-all(bf16[16,4,1024]{2,1,0:T(4,128)(2,1)S(1)} %pad_maximum_fusion.2), channel_id=1, replica_groups=mesh['sample'=16,'block'=2] {'block'}, dimensions={0} | all-to-all | bytes 262144 | tf_op jit(solution)/shard_map/all_to_all | solution.py:202
  530.7 0.7 all_to_all.16
  (211 shorter events, 26.8 us)
Async XLA Ops:
  6.5 5.7 %copy-start = (bf16[1024,16]{0,1:T(8,128)(2,1)S(1)}, bf16[1024,16]{0,1:T(8,128)(2,1)}, u32[]{:S(2)}) copy-start(bf16[1024,16]{0,1:T(8,128)(2,1)} %param.13) | copy-start | bytes 98308
  6.5 236.9 %all-reduce.4.cloned.1.call-start = ((), (), s32[]{:S(2)}) async-start(), calls=%async_computation.1 | async-start | bytes 22020096 | tf_op jit(solution)/shard_map/psum | solution.py:188
  7.9 5.7 %copy-start.10 = (pred[1024]{0:T(1024)(128)(4,1)}, pred[1024]{0:T(1024)(128)(4,1)S(1)}, u32[]{:S(2)}) copy-start(pred[1024]{0:T(1024)(128)(4,1)S(1)} %get-tuple-element.38) | copy-start | bytes 3076
  12.8 0.8 copy-start.14
  32.2 0.9 copy-start.1
  32.2 1.5 copy-start.2
  32.2 3.8 copy-start.15
  32.3 211.1 %copy-start.9 = (f32[128,128]{0,1:T(8,128)}, f32[128,128]{0,1:T(8,128)S(1)}, u32[]{:S(2)}) copy-start(f32[128,128]{0,1:T(8,128)S(1)} %fusion.125) | copy-start | bytes 196612
  35.4 218.4 %copy-start.12 = (pred[2,2]{1,0:T(4,128)(4,1)}, pred[2,2]{1,0:T(4,128)(4,1)S(1)}, u32[]{:S(2)}) copy-start(pred[2,2]{1,0:T(4,128)(4,1)S(1)} %iota_compare_fusion.3) | copy-start | bytes 16
  35.5 218.3 %copy-start.13 = (pred[5,2]{0,1:T(4,128)(4,1)}, pred[5,2]{0,1:T(4,128)(4,1)S(1)}, u32[]{:S(2)}) copy-start(pred[5,2]{0,1:T(4,128)(4,1)S(1)} %iota_compare_fusion.4) | copy-start | bytes 34
  256.4 54.4 %copy-start.7 = (f32[128,128]{1,0:T(8,128)S(1)}, f32[128,128]{1,0:T(8,128)}, u32[]{:S(2)}) copy-start(f32[128,128]{1,0:T(8,128)} %copy.121) | copy-start | bytes 196612
  258.1 54.0 %copy-start.3 = (f32[2,10,128,128]{2,3,0,1:T(8,128)}, f32[2,10,128,128]{2,3,0,1:T(8,128)S(1)}, u32[]{:S(2)}) copy-start(f32[2,10,128,128]{2,3,0,1:T(8,128)S(1)} %multiply_add_fusion.2) | copy-start | bytes 3932164
  312.0 9.3 %copy-start.5 = (f32[2,128,128]{2,1,0:T(8,128)}, f32[2,128,128]{2,1,0:T(8,128)S(1)}, u32[]{:S(2)}) copy-start(f32[2,128,128]{2,1,0:T(8,128)S(1)} %fusion.107) | copy-start | bytes 393220
  312.4 7.2 %copy-start.4 = (f32[2,10,128,128]{2,3,0,1:T(8,128)S(1)}, f32[2,10,128,128]{2,3,0,1:T(8,128)}, u32[]{:S(2)}) copy-start(f32[2,10,128,128]{2,3,0,1:T(8,128)} %copy-done.3) | copy-start | bytes 3932164
  319.3 47.9 %copy-start.8 = (f32[128,128]{1,0:T(8,128)S(1)}, f32[128,128]{1,0:T(8,128)}, u32[]{:S(2)}) copy-start(f32[128,128]{1,0:T(8,128)} %copy.121) | copy-start | bytes 196612
  417.8 53.5 %copy-start.6 = (f32[2,128,128]{2,1,0:T(8,128)S(1)}, f32[2,128,128]{2,1,0:T(8,128)}, u32[]{:S(2)}) copy-start(f32[2,128,128]{2,1,0:T(8,128)} %copy-done.5) | copy-start | bytes 393220
  471.6 6.1 %collective-permute-start = (bf16[2,500,16]{1,2,0:T(8,128)(2,1)S(1)}, bf16[2,500,16]{1,2,0:T(8,128)(2,1)S(1)}, u32[]{:S(2)}, u32[]{:S(2)}) collective-permute-start(bf16[2,500,16]{1,2,0:T(8,128)(2,1)S(1)} %pad_maximum_fusion.3), channel_id=1, source_target_pairs={{0,2},{2,4},{4,6},{6,8},{8,10},{10,12},{12,14},{14,16},{16,18},{18... | collective-permute-start | bytes 96008 | tf_op jit(solution)/shard_map/ppermute | solution.py:18
  477.7 6.1 %collective-permute-start.1 = (bf16[2,500,16]{1,2,0:T(8,128)(2,1)S(1)}, bf16[2,500,16]{1,2,0:T(8,128)(2,1)S(1)}, u32[]{:S(2)}, u32[]{:S(2)}) collective-permute-start(bf16[2,500,16]{1,2,0:T(8,128)(2,1)S(1)} %collective-permute-done), channel_id=1, source_target_pairs={{0,2},{2,4},{4,6},{6,8},{8,10},{10,12},{12,14},{14,16},{16,18},{18... | collective-permute-start | bytes 96008 | tf_op jit(solution)/shard_map/ppermute | solution.py:18
  477.7 6.1 %collective-permute-start.8 = (bf16[2,500,16]{1,2,0:T(8,128)(2,1)S(1)}, bf16[2,500,16]{1,2,0:T(8,128)(2,1)S(1)}, u32[]{:S(2)}, u32[]{:S(2)}) collective-permute-start(bf16[2,500,16]{1,2,0:T(8,128)(2,1)S(1)} %pad_maximum_fusion.3), channel_id=1, source_target_pairs={{0,30},{2,0},{4,2},{6,4},{8,6},{10,8},{12,10},{14,12},{16,14},{18,... | collective-permute-start | bytes 96008 | tf_op jit(solution)/shard_map/ppermute | solution.py:20
  483.8 6.0 %collective-permute-start.2 = (bf16[2,500,16]{1,2,0:T(8,128)(2,1)S(1)}, bf16[2,500,16]{1,2,0:T(8,128)(2,1)S(1)}, u32[]{:S(2)}, u32[]{:S(2)}) collective-permute-start(bf16[2,500,16]{1,2,0:T(8,128)(2,1)S(1)} %collective-permute-done.1), channel_id=1, source_target_pairs={{0,2},{2,4},{4,6},{6,8},{8,10},{10,12},{12,14},{14,16},{16,18},{18... | collective-permute-start | bytes 96008 | tf_op jit(solution)/shard_map/ppermute | solution.py:18
  483.8 6.0 %collective-permute-start.9 = (bf16[2,500,16]{1,2,0:T(8,128)(2,1)S(1)}, bf16[2,500,16]{1,2,0:T(8,128)(2,1)S(1)}, u32[]{:S(2)}, u32[]{:S(2)}) collective-permute-start(bf16[2,500,16]{1,2,0:T(8,128)(2,1)S(1)} %collective-permute-done.8), channel_id=1, source_target_pairs={{0,30},{2,0},{4,2},{6,4},{8,6},{10,8},{12,10},{14,12},{16,14},{18,... | collective-permute-start | bytes 96008 | tf_op jit(solution)/shard_map/ppermute | solution.py:20
  489.8 6.0 %collective-permute-start.3 = (bf16[2,500,16]{1,2,0:T(8,128)(2,1)S(1)}, bf16[2,500,16]{1,2,0:T(8,128)(2,1)S(1)}, u32[]{:S(2)}, u32[]{:S(2)}) collective-permute-start(bf16[2,500,16]{1,2,0:T(8,128)(2,1)S(1)} %collective-permute-done.2), channel_id=1, source_target_pairs={{0,2},{2,4},{4,6},{6,8},{8,10},{10,12},{12,14},{14,16},{16,18},{18... | collective-permute-start | bytes 96008 | tf_op jit(solution)/shard_map/ppermute | solution.py:18
  489.8 6.0 %collective-permute-start.10 = (bf16[2,500,16]{1,2,0:T(8,128)(2,1)S(1)}, bf16[2,500,16]{1,2,0:T(8,128)(2,1)S(1)}, u32[]{:S(2)}, u32[]{:S(2)}) collective-permute-start(bf16[2,500,16]{1,2,0:T(8,128)(2,1)S(1)} %collective-permute-done.9), channel_id=1, source_target_pairs={{0,30},{2,0},{4,2},{6,4},{8,6},{10,8},{12,10},{14,12},{16,14},{18,... | collective-permute-start | bytes 96008 | tf_op jit(solution)/shard_map/ppermute | solution.py:20
  495.9 6.0 %collective-permute-start.4 = (bf16[2,500,16]{1,2,0:T(8,128)(2,1)S(1)}, bf16[2,500,16]{1,2,0:T(8,128)(2,1)S(1)}, u32[]{:S(2)}, u32[]{:S(2)}) collective-permute-start(bf16[2,500,16]{1,2,0:T(8,128)(2,1)S(1)} %collective-permute-done.3), channel_id=1, source_target_pairs={{0,2},{2,4},{4,6},{6,8},{8,10},{10,12},{12,14},{14,16},{16,18},{18... | collective-permute-start | bytes 96008 | tf_op jit(solution)/shard_map/ppermute | solution.py:18
  495.9 6.0 %collective-permute-start.11 = (bf16[2,500,16]{1,2,0:T(8,128)(2,1)S(1)}, bf16[2,500,16]{1,2,0:T(8,128)(2,1)S(1)}, u32[]{:S(2)}, u32[]{:S(2)}) collective-permute-start(bf16[2,500,16]{1,2,0:T(8,128)(2,1)S(1)} %collective-permute-done.10), channel_id=1, source_target_pairs={{0,30},{2,0},{4,2},{6,4},{8,6},{10,8},{12,10},{14,12},{16,14},{18,... | collective-permute-start | bytes 96008 | tf_op jit(solution)/shard_map/ppermute | solution.py:20
  501.9 6.0 %collective-permute-start.5 = (bf16[2,500,16]{1,2,0:T(8,128)(2,1)S(1)}, bf16[2,500,16]{1,2,0:T(8,128)(2,1)S(1)}, u32[]{:S(2)}, u32[]{:S(2)}) collective-permute-start(bf16[2,500,16]{1,2,0:T(8,128)(2,1)S(1)} %collective-permute-done.4), channel_id=1, source_target_pairs={{0,2},{2,4},{4,6},{6,8},{8,10},{10,12},{12,14},{14,16},{16,18},{18... | collective-permute-start | bytes 96008 | tf_op jit(solution)/shard_map/ppermute | solution.py:18
  501.9 6.3 %collective-permute-start.12 = (bf16[2,500,16]{1,2,0:T(8,128)(2,1)S(1)}, bf16[2,500,16]{1,2,0:T(8,128)(2,1)S(1)}, u32[]{:S(2)}, u32[]{:S(2)}) collective-permute-start(bf16[2,500,16]{1,2,0:T(8,128)(2,1)S(1)} %collective-permute-done.11), channel_id=1, source_target_pairs={{0,30},{2,0},{4,2},{6,4},{8,6},{10,8},{12,10},{14,12},{16,14},{18,... | collective-permute-start | bytes 96008 | tf_op jit(solution)/shard_map/ppermute | solution.py:20
  507.9 6.3 %collective-permute-start.6 = (bf16[2,500,16]{1,2,0:T(8,128)(2,1)S(1)}, bf16[2,500,16]{1,2,0:T(8,128)(2,1)S(1)}, u32[]{:S(2)}, u32[]{:S(2)}) collective-permute-start(bf16[2,500,16]{1,2,0:T(8,128)(2,1)S(1)} %collective-permute-done.5), channel_id=1, source_target_pairs={{0,2},{2,4},{4,6},{6,8},{8,10},{10,12},{12,14},{14,16},{16,18},{18... | collective-permute-start | bytes 96008 | tf_op jit(solution)/shard_map/ppermute | solution.py:18
  508.2 6.1 %collective-permute-start.13 = (bf16[2,500,16]{1,2,0:T(8,128)(2,1)S(1)}, bf16[2,500,16]{1,2,0:T(8,128)(2,1)S(1)}, u32[]{:S(2)}, u32[]{:S(2)}) collective-permute-start(bf16[2,500,16]{1,2,0:T(8,128)(2,1)S(1)} %collective-permute-done.12), channel_id=1, source_target_pairs={{0,30},{2,0},{4,2},{6,4},{8,6},{10,8},{12,10},{14,12},{16,14},{18,... | collective-permute-start | bytes 96008 | tf_op jit(solution)/shard_map/ppermute | solution.py:20
  514.2 6.0 %collective-permute-start.7 = (bf16[2,500,16]{1,2,0:T(8,128)(2,1)S(1)}, bf16[2,500,16]{1,2,0:T(8,128)(2,1)S(1)}, u32[]{:S(2)}, u32[]{:S(2)}) collective-permute-start(bf16[2,500,16]{1,2,0:T(8,128)(2,1)S(1)} %collective-permute-done.6), channel_id=1, source_target_pairs={{0,2},{2,4},{4,6},{6,8},{8,10},{10,12},{12,14},{14,16},{16,18},{18... | collective-permute-start | bytes 96008 | tf_op jit(solution)/shard_map/ppermute | solution.py:18
  514.3 6.1 %collective-permute-start.14 = (bf16[2,500,16]{1,2,0:T(8,128)(2,1)S(1)}, bf16[2,500,16]{1,2,0:T(8,128)(2,1)S(1)}, u32[]{:S(2)}, u32[]{:S(2)}) collective-permute-start(bf16[2,500,16]{1,2,0:T(8,128)(2,1)S(1)} %collective-permute-done.13), channel_id=1, source_target_pairs={{0,30},{2,0},{4,2},{6,4},{8,6},{10,8},{12,10},{14,12},{16,14},{18,... | collective-permute-start | bytes 96008 | tf_op jit(solution)/shard_map/ppermute | solution.py:20
  522.5 0.9 copy-start.11
Sparse Core Ops, SparseCore 0:
  32.4 210.9 all-reduce.3
